TPU v7x, 128 devices: a whole 4x4x4 slice. The times are simulated.
128 devices in a mesh: req: 16 (over z, y), exp: 8 (over x, core).
Axes of the slice: x: 4, y: 4, z: 4, core: 2. Of those that a mesh axis runs over, the one named last changes fastest.
Arguments:
- residual: bfloat16 [16384, 2048], P(('req', 'exp')), may hold values from -3 to 3
- query_vectors: bfloat16 [16384, 2048], P(('req', 'exp')), may hold values from -12 to 12
- key_vectors: bfloat16 [16384, 2048], P(('req', 'exp')), may hold values from -12 to 12
- value_vectors: bfloat16 [16384, 2048], P(('req', 'exp')), may hold values from -6 to 6
- segment_ids: int32 [16384], P('req'), may hold values from 0 to 2, as said below
- prompt_lengths: int32 [16, 3], replicated, may hold values from 1 to 512, as said below
- request_groups: int32 [16], replicated, may hold values from 0 to 15, as said below
- page_table: int32 [16, 8], replicated, may hold values from 0 to 127, as said below
- expert_ids: int32 [16384, 8], P(('req', 'exp')), may hold values from 0 to 63, all different within a row; in each aligned block of 128 rows (0 to 127, 128 to 255, ...) at most 24 rows name the same one
- gate_weights: float32 [16384, 8], P(('req', 'exp')), may hold values from 0.1 to 0.6
- out_weight: bfloat16 [2048, 2048], replicated, may hold values from -0.125 to 0.125
- norm_gain: float32 [2048], replicated, may hold values from 0.5 to 2
- expert_inner: bfloat16 [128, 2048, 1024], P(('req', 'exp')), may hold values from -0.125 to 0.125
- expert_outer: bfloat16 [128, 512, 2048], P(('req', 'exp')), may hold values from -0.1875 to 0.1875
Outputs:
- layer_out: bfloat16 [16384, 2048], P(('req', 'exp'))
- kv_pages: bfloat16 [128, 2, 128, 2048], P('req', None, None, 'exp')
Inputs may be any that keep to these rules, and one draw needn't show every extreme that they name: `prompt_lengths`: each row sums to 1024, and its largest entry is 512. `segment_ids`: within each group of 1024 rows the numbers never fall; prompt j of the request r with request_groups[r] = g fills prompt_lengths[r, j] consecutive rows of group g. `request_groups`: each group appears once. `page_table`: all entries differ; the 8 pages of one request lie in 8 different owner groups, the owner of slot s being s // 8. `expert_ids`: the 8 ids of a token differ; among the 128 tokens of one device no expert is named more than 24 times, a bound that some block reaches.
All inputs are finite; a program needn't handle non-finite values.
Results may differ from a plain program's by a relative error of at most 0.013.
Values may be sent and summed in bfloat16 or wider, within the bound.
No kernel may reach another device: no remote copies, remote signals or barrier semaphores. Data moves between devices by JAX's collectives and lax.ppermute only.
A program may use at most 192 MiB of HBM per device.

v0:
```python
import jax
import jax.numpy as jnp
from jax import lax
from jax.sharding import Mesh, PartitionSpec as P

HEAD = 128
PAGE = 128
MEMBER = ("x", "core")
EXPERT_AXES = ("req", "x")
EVERY = ("req", "x", "core")


rope_base = 10000.0
norm_eps = 1e-06
masked_score = -1e30


def partner(value, axis, distance):
    return lax.ppermute(value, axis, [(i, i ^ 1 << distance) for i in range(lax.axis_size(axis))])


def rotate(values_in, positions):
    row_count = values_in.shape[0]
    half_head = HEAD // 2
    inverse = rope_base ** (-(2.0 * jnp.arange(half_head, dtype=jnp.float32)) / HEAD)
    angles = positions[:, None] * inverse[None, :]
    cosine = jnp.cos(angles)[:, None, :]
    sines = jnp.sin(angles)[:, None, :]
    shaped = values_in.astype(jnp.float32).reshape(row_count, -1, HEAD)
    first_half = shaped[..., :half_head]
    second_half = shaped[..., half_head:]
    turned = jnp.concatenate(
        [first_half * cosine - second_half * sines, second_half * cosine + first_half * sines],
        axis=-1,
    )
    return turned.reshape(row_count, -1).astype(jnp.bfloat16)


def score_block(query_block, query_segments, key_block, key_segments):
    scores = jnp.einsum(
        "qhd,khd->hqk", query_block, key_block, preferred_element_type=jnp.float32
    ) * HEAD ** (-0.5)
    same_prompt = (query_segments[:, None] == key_segments[None, :])[None]
    return (jnp.where(same_prompt, scores, masked_score), same_prompt)


def attend_all(query_heads, key_heads, value_heads, group_segments, block_rows):
    block_count = query_heads.shape[0] // block_rows

    def one_block(block_index):
        start_row = block_index * block_rows
        query_block = lax.dynamic_slice_in_dim(query_heads, start_row, block_rows, 0)
        query_segments = lax.dynamic_slice_in_dim(group_segments, start_row, block_rows, 0)
        scores, same_prompt = score_block(query_block, query_segments, key_heads, group_segments)
        top_score = jnp.max(scores, axis=-1, keepdims=True)
        weights = jnp.where(same_prompt, jnp.exp(scores - top_score), 0.0)
        totals = jnp.sum(weights, axis=-1)
        mixed = jnp.einsum(
            "hqk,khd->qhd",
            weights.astype(jnp.bfloat16),
            value_heads,
            preferred_element_type=jnp.float32,
        )
        return (mixed / totals.T[:, :, None]).astype(jnp.bfloat16)

    results = lax.map(one_block, jnp.arange(block_count))
    return results.reshape(query_heads.shape[0], -1)


def send_rows(blocks):
    arrived = lax.all_to_all(blocks, EXPERT_AXES, split_axis=0, concat_axis=0, tiled=True)
    return arrived


def send_back(blocks):
    arrived = lax.all_to_all(blocks, EXPERT_AXES, split_axis=0, concat_axis=0, tiled=True)
    return arrived


def full_expert(rows, inner_both, outer_both):
    projected = jnp.dot(rows, inner_both, preferred_element_type=jnp.float32)
    quarter = projected.shape[1] // 4
    active = jnp.concatenate(
        [
            jax.nn.silu(projected[:, :quarter]) * projected[:, quarter : 2 * quarter],
            jax.nn.silu(projected[:, 2 * quarter : 3 * quarter]) * projected[:, 3 * quarter :],
        ],
        axis=1,
    ).astype(jnp.bfloat16)
    return jnp.dot(active, outer_both, preferred_element_type=jnp.float32).astype(jnp.bfloat16)


def on_device(
    residual,
    query_vectors,
    key_vectors,
    value_vectors,
    segment_ids,
    prompt_lengths,
    request_groups,
    page_table,
    expert_ids,
    gate_weights,
    out_weight,
    norm_gain,
    expert_inner,
    expert_outer,
):
    partner_inner = partner(expert_inner, "core", 0)
    partner_outer = partner(expert_outer, "core", 0)
    tok_rows, model_width = residual.shape
    req_count = lax.axis_size("req")
    member_count = lax.axis_size("x") * lax.axis_size("core")
    device_count = req_count * member_count
    expert_count = device_count // 2
    group_rows = tok_rows * member_count
    top_count = expert_ids.shape[1]
    capacity = 3 * tok_rows * top_count // (2 * expert_count)
    page_count = group_rows // PAGE
    group = lax.axis_index("req")
    member = lax.axis_index(MEMBER)
    holds_request = (request_groups == group).astype(jnp.int32)
    my_lengths = jnp.sum(holds_request[:, None] * prompt_lengths, axis=0)
    my_pages = jnp.sum(holds_request[:, None] * page_table, axis=0)
    starts = jnp.cumsum(my_lengths) - my_lengths
    first_row = member * tok_rows
    my_segments = lax.dynamic_slice_in_dim(segment_ids, first_row, tok_rows, 0)
    prompt_index = jnp.arange(prompt_lengths.shape[1], dtype=jnp.int32)
    token_start = jnp.sum(
        jnp.where(my_segments[:, None] == prompt_index[None, :], starts[None, :], 0), axis=1
    )
    positions = (first_row + jnp.arange(tok_rows, dtype=jnp.int32) - token_start).astype(
        jnp.float32
    )
    query_turned = rotate(query_vectors, positions)
    key_turned = rotate(key_vectors, positions)
    head_chunks = jnp.stack([query_turned, key_turned, value_vectors]).reshape(
        3, tok_rows, member_count, model_width // member_count
    )
    qkv_group = lax.all_to_all(
        head_chunks.transpose(0, 2, 1, 3), MEMBER, split_axis=1, concat_axis=2, tiled=True
    )
    query_group, key_group, value_group = qkv_group[0, 0], qkv_group[1, 0], qkv_group[2, 0]
    column_count = key_group.shape[1]
    stacked = jnp.stack(
        [
            key_group.reshape(page_count, PAGE, column_count),
            value_group.reshape(page_count, PAGE, column_count),
        ],
        axis=1,
    ).reshape(page_count, -1)
    owner_of_page = my_pages // page_count
    group_range = jnp.arange(req_count, dtype=jnp.int32)
    send_select = (owner_of_page[None, :] == group_range[:, None]).astype(jnp.bfloat16)
    outgoing_pages = jnp.dot(send_select, stacked, preferred_element_type=jnp.float32).astype(
        jnp.bfloat16
    )
    incoming_pages = lax.all_to_all(outgoing_pages, "req", split_axis=0, concat_axis=0, tiled=True)
    source_holds = (request_groups[None, :] == group_range[:, None]).astype(jnp.int32)
    source_pages = jnp.sum(source_holds[:, :, None] * page_table[None, :, :], axis=1)
    slot_ids = group * page_count + jnp.arange(page_count, dtype=jnp.int32)
    place_select = jnp.sum(
        (source_pages[None, :, :] == slot_ids[:, None, None]).astype(jnp.int32), axis=2
    ).astype(jnp.bfloat16)
    kv_pages = (
        jnp.dot(place_select, incoming_pages, preferred_element_type=jnp.float32)
        .astype(jnp.bfloat16)
        .reshape(page_count, 2, PAGE, column_count)
    )
    heads_here = column_count // HEAD
    query_heads = query_group.reshape(group_rows, heads_here, HEAD)
    key_heads = key_group.reshape(group_rows, heads_here, HEAD)
    value_heads = value_group.reshape(group_rows, heads_here, HEAD)
    block_rows = group_rows
    attended = attend_all(query_heads, key_heads, value_heads, segment_ids, block_rows)
    token_heads = lax.all_to_all(attended, MEMBER, split_axis=0, concat_axis=1, tiled=True)
    hidden = residual.astype(jnp.float32) + jnp.dot(
        token_heads, out_weight, preferred_element_type=jnp.float32
    )
    normed = (
        hidden * lax.rsqrt(jnp.mean(hidden * hidden, axis=-1, keepdims=True) + norm_eps) * norm_gain
    ).astype(jnp.bfloat16)
    partner_inner, partner_outer, normed = lax.optimization_barrier((partner_inner, partner_outer, normed))
    expert_range = jnp.arange(expert_count, dtype=jnp.int32)
    chosen = (expert_ids[:, :, None] == expert_range[None, None, :]).astype(jnp.int32)
    picked = jnp.sum(chosen, axis=1)
    earlier = jnp.cumsum(picked, axis=0) - picked
    slot_rank = jnp.sum(chosen * earlier[:, None, :], axis=2)
    slot_index = expert_ids * capacity + slot_rank
    slot_range = jnp.arange(expert_count * capacity, dtype=jnp.int32)
    dispatch_matrix = jnp.sum(
        (slot_index[None, :, :] == slot_range[:, None, None]).astype(jnp.int32), axis=2
    ).astype(jnp.bfloat16)
    packed = (
        jnp.dot(dispatch_matrix, normed, preferred_element_type=jnp.float32)
        .astype(jnp.bfloat16)
        .reshape(expert_count, capacity, model_width)
    )
    expert_input = send_rows(packed)
    flat_input = expert_input.reshape(expert_count * capacity, model_width)
    inner_both = jnp.concatenate([expert_inner[0], partner_inner[0]], axis=1)
    outer_both = jnp.concatenate([expert_outer[0], partner_outer[0]], axis=0)
    expert_out = full_expert(flat_input, inner_both, outer_both).reshape(
        expert_count, capacity, model_width
    )
    returned = send_back(expert_out).reshape(expert_count * capacity, model_width)
    combine = jnp.sum(
        jnp.where(slot_index[:, :, None] == slot_range[None, None, :], gate_weights[:, :, None], 0.0),
        axis=1,
    )
    combine_high = combine.astype(jnp.bfloat16)
    combine_low = (combine - combine_high.astype(jnp.float32)).astype(jnp.bfloat16)
    both_parts = jnp.dot(
        jnp.concatenate([combine_high, combine_low], axis=0), returned, preferred_element_type=jnp.float32
    )
    mixed = both_parts[:tok_rows] + both_parts[tok_rows:]
    layer_out = (hidden + mixed).astype(jnp.bfloat16)
    return (layer_out, kv_pages)


def solution(mesh):
    req_count, member_count = mesh.devices.shape
    fine = Mesh(mesh.devices.reshape(req_count, member_count // 2, 2), EVERY)
    token_rows = P(EVERY, None)
    placed = (
        token_rows,
        token_rows,
        token_rows,
        token_rows,
        P("req"),
        P(),
        P(),
        P(),
        token_rows,
        token_rows,
        P(),
        P(),
        P(EVERY, None, None),
        P(EVERY, None, None),
    )
    return jax.shard_map(
        on_device,
        mesh=fine,
        in_specs=placed,
        out_specs=(token_rows, P("req", None, None, MEMBER)),
        check_vma=False,
    )
```

profile of v0, /device:TPU:2, one launch (start us, length us, event | category | flops | bytes accessed | tf_op | source)
XLA Modules:
  0.0 301.3 jit_solution(12466920822962600243)
XLA Ops:
  0.6 1.3 copy.83
  2.0 1.2 copy.81
  5.7 1.2 copy.82
  7.8 1.3 copy.84
  9.0 4.8 %all-to-all-start = ((bf16[3,8,128,256]{2,3,0,1:T(8,128)(2,1)}), bf16[3,8,128,256]{2,3,0,1:T(8,128)(2,1)S(1)}, u32[]{:S(2)}, u32[]{:S(2)}) async-start(bf16[3,8,128,256]{2,3,0,1:T(8,128)(2,1)} %copy.84), calls=%async_computation | async-start | bytes 3145728 | tf_op jit(solution)/shard_map/all_to_all | solution.py:140
  14.8 1.6 broadcast_compare_fusion
  16.4 17.5 %all-to-all-done = bf16[3,8,128,256]{2,3,0,1:T(8,128)(2,1)S(1)} async-done(((bf16[3,8,128,256]{2,3,0,1:T(8,128)(2,1)}), bf16[3,8,128,256]{2,3,0,1:T(8,128)(2,1)S(1)}, u32[]{:S(2)}, u32[]{:S(2)}) %all-to-all-start) | async-done | bytes 1572896 | tf_op jit(solution)/shard_map/all_to_all | solution.py:140
  34.0 1.3 slice_bitcast_fusion.2
  35.6 1.0 reshape_squeeze.9
  37.8 6.1 %fusion.48 = (f32[2,1024]{1,0:T(2,128)S(1)}, bf16[2,1024,1024]{1,2,0:T(8,128)(2,1)}) fusion(pred[1024,1024]{0,1:T(8,128)(4,1)S(1)} %copy-done.1, bf16[1024,2,128]{0,2,1:T(8,128)(2,1)S(1)} %reshape_squeeze.10, bf16[1024,2,128]{0,2,1:T(8,128)(2,1)S(1)} %reshape_squeeze.11), kind=kOutput, calls=%fused_computation.94 | convolution fusion | flops 549454848 | bytes 6299648 | tf_op jit(solution)/shard_map/while/body/eval_jaxpr/sub | solution.py:56
  43.9 2.9 fusion.28
  47.0 0.9 copy.92
  47.8 4.9 %all-to-all-start.1 = ((bf16[8,128,256]{1,2,0:T(8,128)(2,1)}), bf16[8,128,256]{1,2,0:T(8,128)(2,1)S(1)}, u32[]{:S(2)}, u32[]{:S(2)}) async-start(bf16[8,128,256]{1,2,0:T(8,128)(2,1)} %copy.92), calls=%async_computation.1 | async-start | bytes 1048576 | tf_op jit(solution)/shard_map/all_to_all | solution.py:176
  52.7 8.0 %convert_reduce_fusion = s32[1536,128]{1,0:T(8,128)S(1)} fusion(s32[128,8]{0,1:T(8,128)S(1)} %multiply_add_fusion), kind=kLoop, calls=%fused_computation.13 | loop fusion | flops 4521984 | bytes 790528 | tf_op jit(solution)/shard_map/reduce_sum | solution.py:191
  61.6 4.8 %multiply_reduce_fusion = (f32[128]{0:T(128)S(1)}, f32[128,2048]{1,0:T(8,128)S(1)}) fusion(bf16[128,2048]{0,1:T(8,128)(2,1)S(1)} %bitcast.80, bf16[2048,2048]{1,0:T(8,128)(2,1)} %param.24, bf16[128,2048]{1,0:T(8,128)(2,1)} %param.14), kind=kOutput, calls=%fused_computation.45 | convolution fusion | flops 1074790272 | bytes 10486272 | tf_op jit(solution)/shard_map/dot_general | solution.py:177
  66.6 4.4 %convolution_convert_fusion.3 = bf16[1536,2048]{1,0:T(8,128)(2,1)} fusion(bf16[128,2048]{1,0:T(8,128)(2,1)S(1)} %multiply_convert_fusion, s32[1536,128]{1,0:T(8,128)S(1)} %convert_reduce_fusion), kind=kOutput, calls=%fused_computation.11 | convolution fusion | flops 808648704 | bytes 7602176 | tf_op jit(solution)/shard_map/dot_general | solution.py:195
  71.0 11.0 %all-to-all-start.2 = ((bf16[64,24,2048]{2,1,0:T(8,128)(2,1)}), bf16[64,24,2048]{2,1,0:T(8,128)(2,1)}, u32[]{:S(2)}, u32[]{:S(2)}) async-start(bf16[64,24,2048]{2,1,0:T(8,128)(2,1)} %bitcast.73), calls=%async_computation.2 | async-start | bytes 12582912 | tf_op jit(solution)/shard_map/all_to_all | solution.py:71
  84.6 2.9 reduce
  87.5 4.0 %reshape.289 = bf16[16,2,32768]{2,1,0:T(2,128)(2,1)} reshape(bf16[16,65536]{1,0:T(8,128)(2,1)} %reduce) | data formatting | bytes 4194304
  91.5 72.5 %all-to-all-done.2 = bf16[64,24,2048]{2,1,0:T(8,128)(2,1)} async-done(((bf16[64,24,2048]{2,1,0:T(8,128)(2,1)}), bf16[64,24,2048]{2,1,0:T(8,128)(2,1)}, u32[]{:S(2)}, u32[]{:S(2)}) %all-to-all-start.2) | async-done | bytes 6291488 | tf_op jit(solution)/shard_map/all_to_all | solution.py:71
  164.0 9.5 %all-to-all-start.4 = ((bf16[16,2,32768]{2,1,0:T(2,128)(2,1)}), bf16[16,2,32768]{2,1,0:T(2,128)(2,1)S(1)}, u32[]{:S(2)}, u32[]{:S(2)}) async-start(bf16[16,2,32768]{2,1,0:T(2,128)(2,1)} %reshape.289), calls=%async_computation.4 | async-start | bytes 4194304 | tf_op jit(solution)/shard_map/all_to_all | solution.py:158
  173.5 17.9 %fusion.2 = f32[1536,2048]{1,0:T(8,128)S(1)} fusion(bf16[1536,2048]{1,0:T(8,128)(2,1)} %bitcast.13, bf16[2048,1024]{1,0:T(8,128)(2,1)} %bitcast.15, bf16[2048,1024]{1,0:T(8,128)(2,1)} %bitcast.87), kind=kOutput, calls=%fused_computation.4 | convolution fusion | flops 12901679104 | bytes 27262976 | tf_op jit(solution)/shard_map/dot_general | solution.py:81
  191.4 2.2 fusion.16
  193.6 10.2 %convolution_convert_fusion.2 = bf16[1536,2048]{1,0:T(8,128)(2,1)} fusion(bf16[512,2048]{1,0:T(8,128)(2,1)} %bitcast.17, bf16[512,2048]{1,0:T(8,128)(2,1)S(1)} %bitcast.88, bf16[1536,512]{1,0:T(8,128)(2,1)S(1)} %get-tuple-element.39, bf16[1536,512]{1,0:T(8,128)(2,1)S(1)} %get-tuple-element.38), kind=kOutput, calls=%fused_computation.10 | convolution fusion | flops 6460276736 | bytes 13631488 | tf_op jit(solution)/shard_map/dot_general | solution.py:90
  203.8 11.1 %all-to-all-start.3 = ((bf16[64,24,2048]{2,1,0:T(8,128)(2,1)}), bf16[64,24,2048]{2,1,0:T(8,128)(2,1)}, u32[]{:S(2)}, u32[]{:S(2)}) async-start(bf16[64,24,2048]{2,1,0:T(8,128)(2,1)} %bitcast.74), calls=%async_computation.3 | async-start | bytes 12582912 | tf_op jit(solution)/shard_map/all_to_all | solution.py:76
  215.7 2.0 select_reduce_fusion
  218.5 6.7 %reshape.290 = bf16[16,1,65536]{2,1,0:T(2,128)(2,1)} reshape(bf16[16,2,32768]{2,1,0:T(2,128)(2,1)S(1)} %all-to-all-done.4) | data formatting | bytes 4194304
  225.3 4.6 %convolution_convert_fusion.1 = bf16[8,65536]{1,0:T(8,128)(2,1)S(1)} fusion(bf16[16,1,65536]{2,1,0:T(2,128)(2,1)} %reshape.290, s32[8,16]{1,0:T(8,128)S(1)} %convert_reduce_fusion.2), kind=kOutput, calls=%fused_computation.3 | convolution fusion | flops 17301632 | bytes 3146240 | tf_op jit(solution)/shard_map/dot_general | solution.py:166
  229.8 1.2 copy.101
  231.0 64.7 %all-to-all-done.3 = bf16[64,24,2048]{2,1,0:T(8,128)(2,1)} async-done(((bf16[64,24,2048]{2,1,0:T(8,128)(2,1)}), bf16[64,24,2048]{2,1,0:T(8,128)(2,1)}, u32[]{:S(2)}, u32[]{:S(2)}) %all-to-all-start.3) | async-done | bytes 6291488 | tf_op jit(solution)/shard_map/all_to_all | solution.py:76
  295.7 4.6 %fusion.35 = f32[256,2048]{1,0:T(8,128)S(1)} fusion(bf16[1536,2048]{1,0:T(8,128)(2,1)} %bitcast.19, bf16[128,1536]{1,0:T(8,128)(2,1)S(1)} %get-tuple-element.36, bf16[128,1536]{1,0:T(8,128)(2,1)S(1)} %copy-done.3), kind=kOutput, calls=%fused_computation.47 | convolution fusion | flops 1612185600 | bytes 9175040 | tf_op jit(solution)/shard_map/dot_general | solution.py:213
  300.3 1.0 fusion.32
  (70 shorter events, 10.9 us)
Async XLA Ops:
  7.6 6.8 %copy-start.4 = (s32[128,8]{0,1:T(8,128)S(1)}, s32[128,8]{0,1:T(8,128)}, u32[]{:S(2)}) copy-start(s32[128,8]{0,1:T(8,128)} %param.22) | copy-start | bytes 12292
  7.8 7.0 %copy-start.5 = (s32[1024]{0:T(1024)S(1)}, s32[1024]{0:T(1024)}, u32[]{:S(2)}) copy-start(s32[1024]{0:T(1024)} %param.18) | copy-start | bytes 12292
  9.0 24.9 %all-to-all-start = ((bf16[3,8,128,256]{2,3,0,1:T(8,128)(2,1)}), bf16[3,8,128,256]{2,3,0,1:T(8,128)(2,1)S(1)}, u32[]{:S(2)}, u32[]{:S(2)}) async-start(bf16[3,8,128,256]{2,3,0,1:T(8,128)(2,1)} %copy.84), calls=%async_computation | async-start | bytes 3145728 | tf_op jit(solution)/shard_map/all_to_all | solution.py:140
  13.9 52.7 %collective-permute-start = (bf16[1,2048,1024]{2,1,0:T(8,128)(2,1)}, bf16[1,2048,1024]{2,1,0:T(8,128)(2,1)}, u32[]{:S(2)}, u32[]{:S(2)}) collective-permute-start(bf16[1,2048,1024]{2,1,0:T(8,128)(2,1)} %param.26), channel_id=1, source_target_pairs={{0,1},{1,0},{2,3},{3,2},{4,5},{5,4},{6,7},{7,6},{8,9},{9,8},{10,11... | collective-permute-start | bytes 12582920 | tf_op jit(solution)/shard_map/ppermute | solution.py:19
  14.0 52.6 %collective-permute-start.1 = (bf16[1,512,2048]{2,1,0:T(8,128)(2,1)}, bf16[1,512,2048]{2,1,0:T(8,128)(2,1)}, u32[]{:S(2)}, u32[]{:S(2)}) collective-permute-start(bf16[1,512,2048]{2,1,0:T(8,128)(2,1)} %param.27), channel_id=1, source_target_pairs={{0,1},{1,0},{2,3},{3,2},{4,5},{5,4},{6,7},{7,6},{8,9},{9,8},{10,11... | collective-permute-start | bytes 6291464 | tf_op jit(solution)/shard_map/ppermute | solution.py:19
  35.3 2.5 copy-start.1
  37.8 6.1 %copy-start.2 = (bf16[1024,2,128]{0,2,1:T(8,128)(2,1)S(1)}, bf16[1024,2,128]{0,2,1:T(8,128)(2,1)}, u32[]{:S(2)}) copy-start(bf16[1024,2,128]{0,2,1:T(8,128)(2,1)} %reshape_squeeze.9) | copy-start | bytes 1572868
  47.8 13.7 %all-to-all-start.1 = ((bf16[8,128,256]{1,2,0:T(8,128)(2,1)}), bf16[8,128,256]{1,2,0:T(8,128)(2,1)S(1)}, u32[]{:S(2)}, u32[]{:S(2)}) async-start(bf16[8,128,256]{1,2,0:T(8,128)(2,1)} %copy.92), calls=%async_computation.1 | async-start | bytes 1048576 | tf_op jit(solution)/shard_map/all_to_all | solution.py:176
  61.6 4.8 %copy-start.7 = (f32[2048]{0:T(1024)S(1)}, f32[2048]{0:T(1024)}, u32[]{:S(2)}) copy-start(f32[2048]{0:T(1024)} %param.25) | copy-start | bytes 24580
  71.0 11.0 %copy-start.6 = (s32[16,8]{0,1:T(8,128)S(1)}, s32[16,8]{0,1:T(8,128)}, u32[]{:S(2)}) copy-start(s32[16,8]{0,1:T(8,128)} %param.21) | copy-start | bytes 1540
  71.0 11.1 %copy-start = (bf16[8,1,128,256]{2,3,0,1:T(8,128)(2,1)S(1)}, bf16[8,1,128,256]{2,3,0,1:T(8,128)(2,1)}, u32[]{:S(2)}) copy-start(bf16[8,1,128,256]{2,3,0,1:T(8,128)(2,1)} %get-tuple-element.41) | copy-start | bytes 1572868
  71.0 92.9 %all-to-all-start.2 = ((bf16[64,24,2048]{2,1,0:T(8,128)(2,1)}), bf16[64,24,2048]{2,1,0:T(8,128)(2,1)}, u32[]{:S(2)}, u32[]{:S(2)}) async-start(bf16[64,24,2048]{2,1,0:T(8,128)(2,1)} %bitcast.73), calls=%async_computation.2 | async-start | bytes 12582912 | tf_op jit(solution)/shard_map/all_to_all | solution.py:71
  164.0 39.9 %all-to-all-start.4 = ((bf16[16,2,32768]{2,1,0:T(2,128)(2,1)}), bf16[16,2,32768]{2,1,0:T(2,128)(2,1)S(1)}, u32[]{:S(2)}, u32[]{:S(2)}) async-start(bf16[16,2,32768]{2,1,0:T(2,128)(2,1)} %reshape.289), calls=%async_computation.4 | async-start | bytes 4194304 | tf_op jit(solution)/shard_map/all_to_all | solution.py:158
  191.4 2.2 copy-start.10
  203.8 11.2 %copy-start.8 = (f32[128,8]{0,1:T(8,128)S(1)}, f32[128,8]{0,1:T(8,128)}, u32[]{:S(2)}) copy-start(f32[128,8]{0,1:T(8,128)} %param.23) | copy-start | bytes 12292
  203.8 11.3 %copy-start.9 = (s32[16]{0:T(128)S(1)}, s32[16]{0:T(128)}, u32[]{:S(2)}) copy-start(s32[16]{0:T(128)} %param.20) | copy-start | bytes 196
  203.8 91.9 %all-to-all-start.3 = ((bf16[64,24,2048]{2,1,0:T(8,128)(2,1)}), bf16[64,24,2048]{2,1,0:T(8,128)(2,1)}, u32[]{:S(2)}, u32[]{:S(2)}) async-start(bf16[64,24,2048]{2,1,0:T(8,128)(2,1)} %bitcast.74), calls=%async_computation.3 | async-start | bytes 12582912 | tf_op jit(solution)/shard_map/all_to_all | solution.py:76
  225.3 70.4 %copy-start.3 = (bf16[128,1536]{1,0:T(8,128)(2,1)S(1)}, bf16[128,1536]{1,0:T(8,128)(2,1)}, u32[]{:S(2)}) copy-start(bf16[128,1536]{1,0:T(8,128)(2,1)} %get-tuple-element.37) | copy-start | bytes 1179652
where the time goes:
time: 306 us; the launch traced here: 301 us
  waiting for transfers between devices  156 us (51%)
  matrix products  56.2 us (18%)
  starting transfers between devices  41.7 us (14%)
  local copies, waits for them, and re-layouts  24.6 us (8%)
  other arithmetic  22.2 us (7%)
    all_to_all x1, waiting for transfers between devices, send_rows(): lax.all_to_all(blocks, EXPERT_AXES, split_axis=0, concat_axis=0, tiled=True)  72.5 us
    all_to_all x1, waiting for transfers between devices, send_back(): lax.all_to_all(blocks, EXPERT_AXES, split_axis=0, concat_axis=0, tiled=True)  64.7 us
    dot_general x1, matrix products, full_expert(): projected = jnp.dot(rows, inner_both, preferred_element_type=jnp.float32)  17.9 us
    all_to_all x1, waiting for transfers between devices, on_device(): lax.all_to_all(head_chunks.transpose(0, 2, 1, 3), MEMBER, split_axis=1, c...  17.5 us
    unnamed x29, local copies, waits for them, and re-layouts  14.1 us
    all_to_all x1, starting transfers between devices, send_back(): lax.all_to_all(blocks, EXPERT_AXES, split_axis=0, concat_axis=0, tiled=True)  11.1 us
    all_to_all x1, starting transfers between devices, send_rows(): lax.all_to_all(blocks, EXPERT_AXES, split_axis=0, concat_axis=0, tiled=True)  11 us
    dot_general x1, matrix products, full_expert(): jnp.dot(active, outer_both, preferred_element_type=jnp.float32)  10.2 us
  transfers between devices with their start and end apart: 7, of which 4 were waited for; matrix products, arithmetic and copies ran while one was open for 28% of the time, Pallas kernels for 0%

commit v1 on v0

--- a/solution.py
+++ b/solution.py
@@ -151,22 +151,24 @@
     ).reshape(page_count, -1)
     owner_of_page = my_pages // page_count
     group_range = jnp.arange(req_count, dtype=jnp.int32)
-    send_select = (owner_of_page[None, :] == group_range[:, None]).astype(jnp.bfloat16)
-    outgoing_pages = jnp.dot(send_select, stacked, preferred_element_type=jnp.float32).astype(
-        jnp.bfloat16
+    page_range = jnp.arange(page_count, dtype=jnp.int32)
+    page_blocks = stacked.reshape(page_count, 2, PAGE, column_count)
+    sends_to = owner_of_page[None, :] == group_range[:, None]
+    page_for_group = jnp.sum(jnp.where(sends_to, page_range[None, :], 0), axis=1)
+    outgoing_pages = jnp.where(
+        jnp.any(sends_to, axis=1)[:, None, None, None], page_blocks[page_for_group], jnp.zeros_like(page_blocks[:1])
     )
     incoming_pages = lax.all_to_all(outgoing_pages, "req", split_axis=0, concat_axis=0, tiled=True)
     source_holds = (request_groups[None, :] == group_range[:, None]).astype(jnp.int32)
     source_pages = jnp.sum(source_holds[:, :, None] * page_table[None, :, :], axis=1)
-    slot_ids = group * page_count + jnp.arange(page_count, dtype=jnp.int32)
-    place_select = jnp.sum(
-        (source_pages[None, :, :] == slot_ids[:, None, None]).astype(jnp.int32), axis=2
-    ).astype(jnp.bfloat16)
-    kv_pages = (
-        jnp.dot(place_select, incoming_pages, preferred_element_type=jnp.float32)
-        .astype(jnp.bfloat16)
-        .reshape(page_count, 2, PAGE, column_count)
-    )
+    slot_ids = group * page_count + page_range
+    slot_source = jnp.sum(
+        jnp.where(
+            jnp.any(source_pages[None, :, :] == slot_ids[:, None, None], axis=2), group_range[None, :], 0
+        ),
+        axis=1,
+    )
+    kv_pages = incoming_pages[slot_source]
     heads_here = column_count // HEAD
     query_heads = query_group.reshape(group_rows, heads_here, HEAD)
     key_heads = key_group.reshape(group_rows, heads_here, HEAD)

time: 306 us -> 306 us (level)
  waiting for transfers between devices: 156 us -> 170 us
  local copies, waits for them, and re-layouts: 24.6 us -> 12.8 us
  matrix products: 56.2 us -> 52.4 us
    unnamed x29 -> x23, local copies, waits for them, and re-layouts: 14.1 us -> 1.57 us
    all_to_all x1, waiting for transfers between devices: 64.7 us -> 75.4 us  [send_back(): lax.all_to_all(blocks, EXPERT_AXES, split_axis=0, concat_axis=0, tiled=True)]
    dot_general x2 -> x0, matrix products: 5.26 us -> none  [the longest x1 4.57 us: on_device(): jnp.dot(place_select, incoming_pages, preferred_element_type=jnp.float32)]
    all_to_all x1, waiting for transfers between devices: 72.5 us -> 76.5 us  [send_rows(): lax.all_to_all(blocks, EXPERT_AXES, split_axis=0, concat_axis=0, tiled=True)]
    gather x0 -> x2, local copies, waits for them, and re-layouts: none -> 3.56 us  [the longest x1 1.98 us: on_device(): page_blocks[page_for_group]]
    select_n x0 -> x3, other arithmetic: none -> 3.11 us  [the longest x1 3.09 us: on_device(): jnp.where(jnp.any(sends_to, axis=1)[:, None, None, None], page_blocks[pag...]
  transfers between devices with their start and end apart: 7 -> 7, of which waited for: 4 -> 4; matrix products, arithmetic and copies ran while one was open for 28% -> 23% of each run, Pallas kernels for 0% -> 0%
where the time goes in v1:
time: 306 us; the launch traced here: 301 us
  waiting for transfers between devices  170 us (56%)
  matrix products  52.4 us (17%)
  starting transfers between devices  41.7 us (14%)
  other arithmetic  22.7 us (7%)
  local copies, waits for them, and re-layouts  12.8 us (4%)
    all_to_all x1, waiting for transfers between devices, send_rows(): lax.all_to_all(blocks, EXPERT_AXES, split_axis=0, concat_axis=0, tiled=True)  76.5 us
    all_to_all x1, waiting for transfers between devices, send_back(): lax.all_to_all(blocks, EXPERT_AXES, split_axis=0, concat_axis=0, tiled=True)  75.4 us
    dot_general x1, matrix products, full_expert(): projected = jnp.dot(rows, inner_both, preferred_element_type=jnp.float32)  17.9 us
    all_to_all x1, waiting for transfers between devices, on_device(): lax.all_to_all(head_chunks.transpose(0, 2, 1, 3), MEMBER, split_axis=1, c...  17.5 us
    all_to_all x1, starting transfers between devices, send_back(): lax.all_to_all(blocks, EXPERT_AXES, split_axis=0, concat_axis=0, tiled=True)  11.1 us
    all_to_all x1, starting transfers between devices, send_rows(): lax.all_to_all(blocks, EXPERT_AXES, split_axis=0, concat_axis=0, tiled=True)  11 us
    dot_general x1, matrix products, full_expert(): jnp.dot(active, outer_both, preferred_element_type=jnp.float32)  10.2 us
    all_to_all x1, starting transfers between devices, on_device(): lax.all_to_all(outgoing_pages, 'req', split_axis=0, concat_axis=0, tiled=...  9.5 us
  transfers between devices with their start and end apart: 7, of which 4 were waited for; matrix products, arithmetic and copies ran while one was open for 23% of the time, Pallas kernels for 0%

profile of v1, /device:TPU:2, one launch (start us, length us, event | category | flops | bytes accessed | tf_op | source)
XLA Modules:
  0.0 300.9 jit_solution(268669346168221568)
XLA Ops:
  0.6 1.3 copy.79
  2.0 1.2 copy.77
  3.9 0.8 multiply_reduce_fusion.3
  5.7 1.2 copy.78
  7.8 1.6 copy.80
  9.4 4.8 %all-to-all-start = ((bf16[3,8,128,256]{3,2,0,1:T(8,128)(2,1)}), bf16[3,8,128,256]{3,2,0,1:T(8,128)(2,1)S(1)}, u32[]{:S(2)}, u32[]{:S(2)}) async-start(bf16[3,8,128,256]{3,2,0,1:T(8,128)(2,1)} %copy.80), calls=%async_computation | async-start | bytes 3145728 | tf_op jit(solution)/shard_map/all_to_all | solution.py:140
  15.1 1.6 broadcast_compare_fusion
  16.8 17.5 %all-to-all-done = bf16[3,8,128,256]{3,2,0,1:T(8,128)(2,1)S(1)} async-done(((bf16[3,8,128,256]{3,2,0,1:T(8,128)(2,1)}), bf16[3,8,128,256]{3,2,0,1:T(8,128)(2,1)S(1)}, u32[]{:S(2)}, u32[]{:S(2)}) %all-to-all-start) | async-done | bytes 1572896 | tf_op jit(solution)/shard_map/all_to_all | solution.py:140
  34.3 1.3 slice_bitcast_fusion
  36.0 7.5 %fusion.58 = (f32[2,1024]{1,0:T(2,128)S(1)}, bf16[2,1024,1024]{1,2,0:T(8,128)(2,1)}) fusion(pred[1024,1024]{0,1:T(8,128)(4,1)} %broadcast_compare_fusion, bf16[1024,2,128]{2,1,0:T(2,128)(2,1)S(1)} %reshape.324, bf16[1024,2,128]{2,1,0:T(2,128)(2,1)S(1)} %reshape.323), kind=kOutput, calls=%fused_computation.106 | convolution fusion | flops 549454848 | bytes 6299648 | tf_op jit(solution)/shard_map/while/body/eval_jaxpr/sub | solution.py:56
  43.4 3.0 fusion.25
  46.5 0.9 copy.89
  47.4 4.9 %all-to-all-start.1 = ((bf16[8,128,256]{1,2,0:T(8,128)(2,1)}), bf16[8,128,256]{1,2,0:T(8,128)(2,1)S(1)}, u32[]{:S(2)}, u32[]{:S(2)}) async-start(bf16[8,128,256]{1,2,0:T(8,128)(2,1)} %copy.89), calls=%async_computation.1 | async-start | bytes 1048576 | tf_op jit(solution)/shard_map/all_to_all | solution.py:178
  52.3 8.0 %convert_reduce_fusion = s32[1536,128]{1,0:T(8,128)S(1)} fusion(s32[128,8]{0,1:T(8,128)S(1)} %multiply_add_fusion), kind=kLoop, calls=%fused_computation.12 | loop fusion | flops 4521984 | bytes 790528 | tf_op jit(solution)/shard_map/reduce_sum | solution.py:193
  60.3 0.8 all-to-all-done.1
  61.1 4.8 %multiply_reduce_fusion = (f32[128]{0:T(128)S(1)}, f32[128,2048]{1,0:T(8,128)S(1)}) fusion(bf16[128,2048]{0,1:T(8,128)(2,1)S(1)} %bitcast.69, bf16[2048,2048]{1,0:T(8,128)(2,1)} %param.24, bf16[128,2048]{1,0:T(8,128)(2,1)S(1)} %copy-done.2), kind=kOutput, calls=%fused_computation.43 | convolution fusion | flops 1074790272 | bytes 10486272 | tf_op jit(solution)/shard_map/dot_general | solution.py:179
  66.1 4.4 %convolution_convert_fusion.1 = bf16[1536,2048]{1,0:T(8,128)(2,1)} fusion(bf16[128,2048]{1,0:T(8,128)(2,1)S(1)} %multiply_convert_fusion, s32[1536,128]{1,0:T(8,128)S(1)} %convert_reduce_fusion), kind=kOutput, calls=%fused_computation.10 | convolution fusion | flops 808648704 | bytes 7602176 | tf_op jit(solution)/shard_map/dot_general | solution.py:197
  70.5 11.0 %all-to-all-start.2 = ((bf16[64,24,2048]{2,1,0:T(8,128)(2,1)}), bf16[64,24,2048]{2,1,0:T(8,128)(2,1)}, u32[]{:S(2)}, u32[]{:S(2)}) async-start(bf16[64,24,2048]{2,1,0:T(8,128)(2,1)} %bitcast.65), calls=%async_computation.2 | async-start | bytes 12582912 | tf_op jit(solution)/shard_map/all_to_all | solution.py:71
  82.0 2.0 gather_fusion
  83.9 3.1 %broadcast_select_fusion = bf16[16,2,128,256]{3,2,1,0:T(8,128)(2,1)} fusion(bf16[16,2,128,256]{3,2,1,0:T(8,128)(2,1)} %gather_fusion, pred[16]{0:T(512)(128)(4,1)S(1)} %fusion.50), kind=kLoop, calls=%fused_computation.33 | loop fusion | flops 1048576 | bytes 4194320 | tf_op jit(solution)/shard_map/jit(_where)/select_n | solution.py:158
  87.0 76.5 %all-to-all-done.2 = bf16[64,24,2048]{2,1,0:T(8,128)(2,1)} async-done(((bf16[64,24,2048]{2,1,0:T(8,128)(2,1)}), bf16[64,24,2048]{2,1,0:T(8,128)(2,1)}, u32[]{:S(2)}, u32[]{:S(2)}) %all-to-all-start.2) | async-done | bytes 6291488 | tf_op jit(solution)/shard_map/all_to_all | solution.py:71
  163.5 9.5 %all-to-all-start.4 = ((bf16[16,2,128,256]{3,2,1,0:T(8,128)(2,1)}), bf16[16,2,128,256]{3,2,1,0:T(8,128)(2,1)S(1)}, u32[]{:S(2)}, u32[]{:S(2)}) async-start(bf16[16,2,128,256]{3,2,1,0:T(8,128)(2,1)} %broadcast_select_fusion), calls=%async_computation.4 | async-start | bytes 4194304 | tf_op jit(solution)/shard_map/all_to_all | solution.py:161
  173.0 17.9 %fusion.1 = f32[1536,2048]{1,0:T(8,128)S(1)} fusion(bf16[1536,2048]{1,0:T(8,128)(2,1)} %bitcast.13, bf16[2048,1024]{1,0:T(8,128)(2,1)} %bitcast.15, bf16[2048,1024]{1,0:T(8,128)(2,1)} %bitcast.76), kind=kOutput, calls=%fused_computation.3 | convolution fusion | flops 12901679104 | bytes 27262976 | tf_op jit(solution)/shard_map/dot_general | solution.py:81
  190.9 2.2 fusion.15
  193.1 10.2 %convolution_convert_fusion = bf16[1536,2048]{1,0:T(8,128)(2,1)} fusion(bf16[512,2048]{1,0:T(8,128)(2,1)} %bitcast.17, bf16[512,2048]{1,0:T(8,128)(2,1)S(1)} %bitcast.77, bf16[1536,512]{1,0:T(8,128)(2,1)S(1)} %get-tuple-element.29, bf16[1536,512]{1,0:T(8,128)(2,1)S(1)} %get-tuple-element.28), kind=kOutput, calls=%fused_computation.9 | convolution fusion | flops 6460276736 | bytes 13631488 | tf_op jit(solution)/shard_map/dot_general | solution.py:90
  203.4 11.1 %all-to-all-start.3 = ((bf16[64,24,2048]{2,1,0:T(8,128)(2,1)}), bf16[64,24,2048]{2,1,0:T(8,128)(2,1)}, u32[]{:S(2)}, u32[]{:S(2)}) async-start(bf16[64,24,2048]{2,1,0:T(8,128)(2,1)} %bitcast.66), calls=%async_computation.3 | async-start | bytes 12582912 | tf_op jit(solution)/shard_map/all_to_all | solution.py:76
  215.3 2.0 select_reduce_fusion
  217.4 0.8 subtract_convert_fusion
  218.2 1.6 gather_fusion.1
  219.8 75.4 %all-to-all-done.3 = bf16[64,24,2048]{2,1,0:T(8,128)(2,1)} async-done(((bf16[64,24,2048]{2,1,0:T(8,128)(2,1)}), bf16[64,24,2048]{2,1,0:T(8,128)(2,1)}, u32[]{:S(2)}, u32[]{:S(2)}) %all-to-all-start.3) | async-done | bytes 6291488 | tf_op jit(solution)/shard_map/all_to_all | solution.py:76
  295.1 4.7 %fusion.32 = f32[256,2048]{1,0:T(8,128)S(1)} fusion(bf16[1536,2048]{1,0:T(8,128)(2,1)} %bitcast.19, bf16[128,1536]{1,0:T(8,128)(2,1)S(1)} %get-tuple-element.26, bf16[128,1536]{1,0:T(8,128)(2,1)} %get-tuple-element.27), kind=kOutput, calls=%fused_computation.45 | convolution fusion | flops 1612185600 | bytes 9175040 | tf_op jit(solution)/shard_map/dot_general | solution.py:215
  299.9 1.0 fusion.29
  (66 shorter events, 5.4 us)
Async XLA Ops:
  7.6 7.1 %copy-start.3 = (s32[128,8]{0,1:T(8,128)S(1)}, s32[128,8]{0,1:T(8,128)}, u32[]{:S(2)}) copy-start(s32[128,8]{0,1:T(8,128)} %param.22) | copy-start | bytes 12292
  7.8 7.4 %copy-start.4 = (s32[1024]{0:T(1024)S(1)}, s32[1024]{0:T(1024)}, u32[]{:S(2)}) copy-start(s32[1024]{0:T(1024)} %param.18) | copy-start | bytes 12292
  9.4 24.9 %all-to-all-start = ((bf16[3,8,128,256]{3,2,0,1:T(8,128)(2,1)}), bf16[3,8,128,256]{3,2,0,1:T(8,128)(2,1)S(1)}, u32[]{:S(2)}, u32[]{:S(2)}) async-start(bf16[3,8,128,256]{3,2,0,1:T(8,128)(2,1)} %copy.80), calls=%async_computation | async-start | bytes 3145728 | tf_op jit(solution)/shard_map/all_to_all | solution.py:140
  14.2 51.9 %collective-permute-start = (bf16[1,2048,1024]{2,1,0:T(8,128)(2,1)}, bf16[1,2048,1024]{2,1,0:T(8,128)(2,1)}, u32[]{:S(2)}, u32[]{:S(2)}) collective-permute-start(bf16[1,2048,1024]{2,1,0:T(8,128)(2,1)} %param.26), channel_id=1, source_target_pairs={{0,1},{1,0},{2,3},{3,2},{4,5},{5,4},{6,7},{7,6},{8,9},{9,8},{10,11... | collective-permute-start | bytes 12582920 | tf_op jit(solution)/shard_map/ppermute | solution.py:19
  14.3 51.8 %collective-permute-start.1 = (bf16[1,512,2048]{2,1,0:T(8,128)(2,1)}, bf16[1,512,2048]{2,1,0:T(8,128)(2,1)}, u32[]{:S(2)}, u32[]{:S(2)}) collective-permute-start(bf16[1,512,2048]{2,1,0:T(8,128)(2,1)} %param.27), channel_id=1, source_target_pairs={{0,1},{1,0},{2,3},{3,2},{4,5},{5,4},{6,7},{7,6},{8,9},{9,8},{10,11... | collective-permute-start | bytes 6291464 | tf_op jit(solution)/shard_map/ppermute | solution.py:19
  46.4 14.7 %copy-start.2 = (bf16[128,2048]{1,0:T(8,128)(2,1)S(1)}, bf16[128,2048]{1,0:T(8,128)(2,1)}, u32[]{:S(2)}) copy-start(bf16[128,2048]{1,0:T(8,128)(2,1)} %param.14) | copy-start | bytes 1572868
  47.4 13.8 %all-to-all-start.1 = ((bf16[8,128,256]{1,2,0:T(8,128)(2,1)}), bf16[8,128,256]{1,2,0:T(8,128)(2,1)S(1)}, u32[]{:S(2)}, u32[]{:S(2)}) async-start(bf16[8,128,256]{1,2,0:T(8,128)(2,1)} %copy.89), calls=%async_computation.1 | async-start | bytes 1048576 | tf_op jit(solution)/shard_map/all_to_all | solution.py:178
  61.1 4.8 %copy-start.6 = (f32[2048]{0:T(1024)S(1)}, f32[2048]{0:T(1024)}, u32[]{:S(2)}) copy-start(f32[2048]{0:T(1024)} %param.25) | copy-start | bytes 24580
  70.5 11.0 %copy-start.5 = (s32[16,8]{0,1:T(8,128)S(1)}, s32[16,8]{0,1:T(8,128)}, u32[]{:S(2)}) copy-start(s32[16,8]{0,1:T(8,128)} %param.21) | copy-start | bytes 1540
  70.5 11.3 %copy-start = (bf16[8,1,128,256]{3,2,1,0:T(8,128)(2,1)S(1)}, bf16[8,1,128,256]{3,2,1,0:T(8,128)(2,1)}, u32[]{:S(2)}) copy-start(bf16[8,1,128,256]{3,2,1,0:T(8,128)(2,1)} %get-tuple-element.30) | copy-start | bytes 1572868
  70.5 11.3 %copy-start.1 = (bf16[8,1,128,256]{3,2,1,0:T(8,128)(2,1)S(1)}, bf16[8,1,128,256]{3,2,1,0:T(8,128)(2,1)}, u32[]{:S(2)}) copy-start(bf16[8,1,128,256]{3,2,1,0:T(8,128)(2,1)} %get-tuple-element.31) | copy-start | bytes 1572868
  70.5 92.9 %all-to-all-start.2 = ((bf16[64,24,2048]{2,1,0:T(8,128)(2,1)}), bf16[64,24,2048]{2,1,0:T(8,128)(2,1)}, u32[]{:S(2)}, u32[]{:S(2)}) async-start(bf16[64,24,2048]{2,1,0:T(8,128)(2,1)} %bitcast.65), calls=%async_computation.2 | async-start | bytes 12582912 | tf_op jit(solution)/shard_map/all_to_all | solution.py:71
  163.5 39.9 %all-to-all-start.4 = ((bf16[16,2,128,256]{3,2,1,0:T(8,128)(2,1)}), bf16[16,2,128,256]{3,2,1,0:T(8,128)(2,1)S(1)}, u32[]{:S(2)}, u32[]{:S(2)}) async-start(bf16[16,2,128,256]{3,2,1,0:T(8,128)(2,1)} %broadcast_select_fusion), calls=%async_computation.4 | async-start | bytes 4194304 | tf_op jit(solution)/shard_map/all_to_all | solution.py:161
  190.9 2.2 copy-start.9
  203.3 11.2 %copy-start.7 = (f32[128,8]{0,1:T(8,128)S(1)}, f32[128,8]{0,1:T(8,128)}, u32[]{:S(2)}) copy-start(f32[128,8]{0,1:T(8,128)} %param.23) | copy-start | bytes 12292
  203.3 11.3 %copy-start.8 = (s32[16]{0:T(128)S(1)}, s32[16]{0:T(128)}, u32[]{:S(2)}) copy-start(s32[16]{0:T(128)} %param.20) | copy-start | bytes 196
  203.4 91.8 %all-to-all-start.3 = ((bf16[64,24,2048]{2,1,0:T(8,128)(2,1)}), bf16[64,24,2048]{2,1,0:T(8,128)(2,1)}, u32[]{:S(2)}, u32[]{:S(2)}) async-start(bf16[64,24,2048]{2,1,0:T(8,128)(2,1)} %bitcast.66), calls=%async_computation.3 | async-start | bytes 12582912 | tf_op jit(solution)/shard_map/all_to_all | solution.py:76

commit v2 on v1

--- a/solution.py
+++ b/solution.py
@@ -210,12 +210,7 @@
         jnp.where(slot_index[:, :, None] == slot_range[None, None, :], gate_weights[:, :, None], 0.0),
         axis=1,
     )
-    combine_high = combine.astype(jnp.bfloat16)
-    combine_low = (combine - combine_high.astype(jnp.float32)).astype(jnp.bfloat16)
-    both_parts = jnp.dot(
-        jnp.concatenate([combine_high, combine_low], axis=0), returned, preferred_element_type=jnp.float32
-    )
-    mixed = both_parts[:tok_rows] + both_parts[tok_rows:]
+    mixed = jnp.dot(combine.astype(jnp.bfloat16), returned, preferred_element_type=jnp.float32)
     layer_out = (hidden + mixed).astype(jnp.bfloat16)
     return (layer_out, kv_pages)
 

time: 306 us -> 305 us (level)
  no operation moved by 1% of the time
where the time goes in v2:
time: 305 us; the launch traced here: 300 us
  waiting for transfers between devices  169 us (55%)
  matrix products  52.3 us (17%)
  starting transfers between devices  41.7 us (14%)
  other arithmetic  21.7 us (7%)
  local copies, waits for them, and re-layouts  14.1 us (5%)
    all_to_all x1, waiting for transfers between devices, send_rows(): lax.all_to_all(blocks, EXPERT_AXES, split_axis=0, concat_axis=0, tiled=True)  76.5 us
    all_to_all x1, waiting for transfers between devices, send_back(): lax.all_to_all(blocks, EXPERT_AXES, split_axis=0, concat_axis=0, tiled=True)  74.2 us
    dot_general x1, matrix products, full_expert(): projected = jnp.dot(rows, inner_both, preferred_element_type=jnp.float32)  17.9 us
    all_to_all x1, waiting for transfers between devices, on_device(): lax.all_to_all(head_chunks.transpose(0, 2, 1, 3), MEMBER, split_axis=1, c...  17.5 us
    all_to_all x1, starting transfers between devices, send_back(): lax.all_to_all(blocks, EXPERT_AXES, split_axis=0, concat_axis=0, tiled=True)  11.1 us
    all_to_all x1, starting transfers between devices, send_rows(): lax.all_to_all(blocks, EXPERT_AXES, split_axis=0, concat_axis=0, tiled=True)  11 us
    dot_general x1, matrix products, full_expert(): jnp.dot(active, outer_both, preferred_element_type=jnp.float32)  10.2 us
    all_to_all x1, starting transfers between devices, on_device(): lax.all_to_all(outgoing_pages, 'req', split_axis=0, concat_axis=0, tiled=...  9.5 us
  transfers between devices with their start and end apart: 7, of which 4 were waited for; matrix products, arithmetic and copies ran while one was open for 23% of the time, Pallas kernels for 0%

profile of v2, /device:TPU:2, one launch (start us, length us, event | category | flops | bytes accessed | tf_op | source)
XLA Modules:
  0.0 299.7 jit_solution(13555395175620390379)
XLA Ops:
  0.6 1.3 copy.79
  2.0 1.2 copy.77
  3.9 0.8 multiply_reduce_fusion.3
  4.9 0.8 dynamic_slice.10
  5.7 1.2 copy.78
  7.8 1.6 copy.80
  9.4 4.8 %all-to-all-start = ((bf16[3,8,128,256]{3,2,0,1:T(8,128)(2,1)}), bf16[3,8,128,256]{3,2,0,1:T(8,128)(2,1)S(1)}, u32[]{:S(2)}, u32[]{:S(2)}) async-start(bf16[3,8,128,256]{3,2,0,1:T(8,128)(2,1)} %copy.80), calls=%async_computation | async-start | bytes 3145728 | tf_op jit(solution)/shard_map/all_to_all | solution.py:140
  15.1 1.6 broadcast_compare_fusion
  16.8 17.5 %all-to-all-done = bf16[3,8,128,256]{3,2,0,1:T(8,128)(2,1)S(1)} async-done(((bf16[3,8,128,256]{3,2,0,1:T(8,128)(2,1)}), bf16[3,8,128,256]{3,2,0,1:T(8,128)(2,1)S(1)}, u32[]{:S(2)}, u32[]{:S(2)}) %all-to-all-start) | async-done | bytes 1572896 | tf_op jit(solution)/shard_map/all_to_all | solution.py:140
  34.3 1.3 slice_bitcast_fusion
  36.0 7.5 %fusion.53 = (f32[2,1024]{1,0:T(2,128)S(1)}, bf16[2,1024,1024]{1,2,0:T(8,128)(2,1)}) fusion(pred[1024,1024]{0,1:T(8,128)(4,1)} %broadcast_compare_fusion, bf16[1024,2,128]{2,1,0:T(2,128)(2,1)S(1)} %reshape.324, bf16[1024,2,128]{2,1,0:T(2,128)(2,1)S(1)} %reshape.323), kind=kOutput, calls=%fused_computation.100 | convolution fusion | flops 549454848 | bytes 6299648 | tf_op jit(solution)/shard_map/while/body/eval_jaxpr/sub | solution.py:56
  43.4 3.0 fusion.26
  46.5 0.9 copy.89
  47.4 4.9 %all-to-all-start.1 = ((bf16[8,128,256]{1,2,0:T(8,128)(2,1)}), bf16[8,128,256]{1,2,0:T(8,128)(2,1)S(1)}, u32[]{:S(2)}, u32[]{:S(2)}) async-start(bf16[8,128,256]{1,2,0:T(8,128)(2,1)} %copy.89), calls=%async_computation.1 | async-start | bytes 1048576 | tf_op jit(solution)/shard_map/all_to_all | solution.py:178
  52.3 8.0 %convert_reduce_fusion = s32[1536,128]{1,0:T(8,128)S(1)} fusion(s32[128,8]{0,1:T(8,128)S(1)} %multiply_add_fusion), kind=kLoop, calls=%fused_computation.12 | loop fusion | flops 4521984 | bytes 790528 | tf_op jit(solution)/shard_map/reduce_sum | solution.py:193
  60.3 0.8 all-to-all-done.1
  61.1 4.8 %multiply_reduce_fusion = (f32[128]{0:T(128)S(1)}, f32[128,2048]{1,0:T(8,128)S(1)}) fusion(bf16[128,2048]{0,1:T(8,128)(2,1)S(1)} %bitcast.70, bf16[2048,2048]{1,0:T(8,128)(2,1)} %param.24, bf16[128,2048]{1,0:T(8,128)(2,1)S(1)} %copy-done.2), kind=kOutput, calls=%fused_computation.42 | convolution fusion | flops 1074790272 | bytes 10486272 | tf_op jit(solution)/shard_map/dot_general | solution.py:179
  66.1 4.4 %convolution_convert_fusion.1 = bf16[1536,2048]{1,0:T(8,128)(2,1)} fusion(bf16[128,2048]{1,0:T(8,128)(2,1)S(1)} %multiply_convert_fusion, s32[1536,128]{1,0:T(8,128)S(1)} %convert_reduce_fusion), kind=kOutput, calls=%fused_computation.10 | convolution fusion | flops 808648704 | bytes 7602176 | tf_op jit(solution)/shard_map/dot_general | solution.py:197
  70.5 11.0 %all-to-all-start.2 = ((bf16[64,24,2048]{2,1,0:T(8,128)(2,1)}), bf16[64,24,2048]{2,1,0:T(8,128)(2,1)}, u32[]{:S(2)}, u32[]{:S(2)}) async-start(bf16[64,24,2048]{2,1,0:T(8,128)(2,1)} %bitcast.66), calls=%async_computation.2 | async-start | bytes 12582912 | tf_op jit(solution)/shard_map/all_to_all | solution.py:71
  82.0 2.0 gather_fusion
  83.9 3.1 %broadcast_select_fusion = bf16[16,2,128,256]{3,2,1,0:T(8,128)(2,1)} fusion(bf16[16,2,128,256]{3,2,1,0:T(8,128)(2,1)} %gather_fusion, pred[16]{0:T(512)(128)(4,1)S(1)} %fusion.46), kind=kLoop, calls=%fused_computation.35 | loop fusion | flops 1048576 | bytes 4194320 | tf_op jit(solution)/shard_map/jit(_where)/select_n | solution.py:158
  87.0 76.5 %all-to-all-done.2 = bf16[64,24,2048]{2,1,0:T(8,128)(2,1)} async-done(((bf16[64,24,2048]{2,1,0:T(8,128)(2,1)}), bf16[64,24,2048]{2,1,0:T(8,128)(2,1)}, u32[]{:S(2)}, u32[]{:S(2)}) %all-to-all-start.2) | async-done | bytes 6291488 | tf_op jit(solution)/shard_map/all_to_all | solution.py:71
  163.5 9.5 %all-to-all-start.4 = ((bf16[16,2,128,256]{3,2,1,0:T(8,128)(2,1)}), bf16[16,2,128,256]{3,2,1,0:T(8,128)(2,1)S(1)}, u32[]{:S(2)}, u32[]{:S(2)}) async-start(bf16[16,2,128,256]{3,2,1,0:T(8,128)(2,1)} %broadcast_select_fusion), calls=%async_computation.4 | async-start | bytes 4194304 | tf_op jit(solution)/shard_map/all_to_all | solution.py:161
  173.0 17.9 %fusion.1 = f32[1536,2048]{1,0:T(8,128)S(1)} fusion(bf16[1536,2048]{1,0:T(8,128)(2,1)} %bitcast.13, bf16[2048,1024]{1,0:T(8,128)(2,1)} %bitcast.15, bf16[2048,1024]{1,0:T(8,128)(2,1)} %bitcast.77), kind=kOutput, calls=%fused_computation.3 | convolution fusion | flops 12901679104 | bytes 27262976 | tf_op jit(solution)/shard_map/dot_general | solution.py:81
  190.9 2.2 fusion.15
  193.1 10.2 %convolution_convert_fusion = bf16[1536,2048]{1,0:T(8,128)(2,1)} fusion(bf16[512,2048]{1,0:T(8,128)(2,1)} %bitcast.17, bf16[512,2048]{1,0:T(8,128)(2,1)S(1)} %bitcast.78, bf16[1536,512]{1,0:T(8,128)(2,1)S(1)} %get-tuple-element.27, bf16[1536,512]{1,0:T(8,128)(2,1)S(1)} %get-tuple-element.26), kind=kOutput, calls=%fused_computation.9 | convolution fusion | flops 6460276736 | bytes 13631488 | tf_op jit(solution)/shard_map/dot_general | solution.py:90
  203.4 11.1 %all-to-all-start.3 = ((bf16[64,24,2048]{2,1,0:T(8,128)(2,1)}), bf16[64,24,2048]{2,1,0:T(8,128)(2,1)}, u32[]{:S(2)}, u32[]{:S(2)}) async-start(bf16[64,24,2048]{2,1,0:T(8,128)(2,1)} %bitcast.67), calls=%async_computation.3 | async-start | bytes 12582912 | tf_op jit(solution)/shard_map/all_to_all | solution.py:76
  214.4 0.7 copy.93
  216.6 2.9 select_reduce_fusion
  219.4 1.6 gather_fusion.1
  221.0 74.2 %all-to-all-done.3 = bf16[64,24,2048]{2,1,0:T(8,128)(2,1)} async-done(((bf16[64,24,2048]{2,1,0:T(8,128)(2,1)}), bf16[64,24,2048]{2,1,0:T(8,128)(2,1)}, u32[]{:S(2)}, u32[]{:S(2)}) %all-to-all-start.3) | async-done | bytes 6291488 | tf_op jit(solution)/shard_map/all_to_all | solution.py:76
  295.2 4.6 %fusion.19 = bf16[128,2048]{1,0:T(8,128)(2,1)} fusion(f32[128,2048]{1,0:T(8,128)S(1)} %get-tuple-element.44, bf16[1536,2048]{1,0:T(8,128)(2,1)} %bitcast.19, bf16[128,1536]{1,0:T(8,128)(2,1)S(1)} %select_reduce_fusion), kind=kOutput, calls=%fused_computation.33 | convolution fusion | flops 805830656 | bytes 8257536 | tf_op jit(solution)/shard_map/dot_general | solution.py:213
  (64 shorter events, 5.1 us)
Async XLA Ops:
  7.6 7.1 %copy-start.3 = (s32[128,8]{0,1:T(8,128)S(1)}, s32[128,8]{0,1:T(8,128)}, u32[]{:S(2)}) copy-start(s32[128,8]{0,1:T(8,128)} %param.22) | copy-start | bytes 12292
  7.8 7.4 %copy-start.4 = (s32[1024]{0:T(1024)S(1)}, s32[1024]{0:T(1024)}, u32[]{:S(2)}) copy-start(s32[1024]{0:T(1024)} %param.18) | copy-start | bytes 12292
  9.4 24.9 %all-to-all-start = ((bf16[3,8,128,256]{3,2,0,1:T(8,128)(2,1)}), bf16[3,8,128,256]{3,2,0,1:T(8,128)(2,1)S(1)}, u32[]{:S(2)}, u32[]{:S(2)}) async-start(bf16[3,8,128,256]{3,2,0,1:T(8,128)(2,1)} %copy.80), calls=%async_computation | async-start | bytes 3145728 | tf_op jit(solution)/shard_map/all_to_all | solution.py:140
  14.2 51.9 %collective-permute-start = (bf16[1,2048,1024]{2,1,0:T(8,128)(2,1)}, bf16[1,2048,1024]{2,1,0:T(8,128)(2,1)}, u32[]{:S(2)}, u32[]{:S(2)}) collective-permute-start(bf16[1,2048,1024]{2,1,0:T(8,128)(2,1)} %param.26), channel_id=1, source_target_pairs={{0,1},{1,0},{2,3},{3,2},{4,5},{5,4},{6,7},{7,6},{8,9},{9,8},{10,11... | collective-permute-start | bytes 12582920 | tf_op jit(solution)/shard_map/ppermute | solution.py:19
  14.3 51.8 %collective-permute-start.1 = (bf16[1,512,2048]{2,1,0:T(8,128)(2,1)}, bf16[1,512,2048]{2,1,0:T(8,128)(2,1)}, u32[]{:S(2)}, u32[]{:S(2)}) collective-permute-start(bf16[1,512,2048]{2,1,0:T(8,128)(2,1)} %param.27), channel_id=1, source_target_pairs={{0,1},{1,0},{2,3},{3,2},{4,5},{5,4},{6,7},{7,6},{8,9},{9,8},{10,11... | collective-permute-start | bytes 6291464 | tf_op jit(solution)/shard_map/ppermute | solution.py:19
  46.4 14.8 %copy-start.2 = (bf16[128,2048]{1,0:T(8,128)(2,1)S(1)}, bf16[128,2048]{1,0:T(8,128)(2,1)}, u32[]{:S(2)}) copy-start(bf16[128,2048]{1,0:T(8,128)(2,1)} %param.14) | copy-start | bytes 1572868
  47.4 13.8 %all-to-all-start.1 = ((bf16[8,128,256]{1,2,0:T(8,128)(2,1)}), bf16[8,128,256]{1,2,0:T(8,128)(2,1)S(1)}, u32[]{:S(2)}, u32[]{:S(2)}) async-start(bf16[8,128,256]{1,2,0:T(8,128)(2,1)} %copy.89), calls=%async_computation.1 | async-start | bytes 1048576 | tf_op jit(solution)/shard_map/all_to_all | solution.py:178
  61.1 4.8 %copy-start.6 = (f32[2048]{0:T(1024)S(1)}, f32[2048]{0:T(1024)}, u32[]{:S(2)}) copy-start(f32[2048]{0:T(1024)} %param.25) | copy-start | bytes 24580
  70.5 11.0 %copy-start.5 = (s32[16,8]{0,1:T(8,128)S(1)}, s32[16,8]{0,1:T(8,128)}, u32[]{:S(2)}) copy-start(s32[16,8]{0,1:T(8,128)} %param.21) | copy-start | bytes 1540
  70.5 11.3 %copy-start = (bf16[8,1,128,256]{3,2,1,0:T(8,128)(2,1)S(1)}, bf16[8,1,128,256]{3,2,1,0:T(8,128)(2,1)}, u32[]{:S(2)}) copy-start(bf16[8,1,128,256]{3,2,1,0:T(8,128)(2,1)} %get-tuple-element.28) | copy-start | bytes 1572868
  70.5 11.3 %copy-start.1 = (bf16[8,1,128,256]{3,2,1,0:T(8,128)(2,1)S(1)}, bf16[8,1,128,256]{3,2,1,0:T(8,128)(2,1)}, u32[]{:S(2)}) copy-start(bf16[8,1,128,256]{3,2,1,0:T(8,128)(2,1)} %get-tuple-element.29) | copy-start | bytes 1572868
  70.5 92.9 %all-to-all-start.2 = ((bf16[64,24,2048]{2,1,0:T(8,128)(2,1)}), bf16[64,24,2048]{2,1,0:T(8,128)(2,1)}, u32[]{:S(2)}, u32[]{:S(2)}) async-start(bf16[64,24,2048]{2,1,0:T(8,128)(2,1)} %bitcast.66), calls=%async_computation.2 | async-start | bytes 12582912 | tf_op jit(solution)/shard_map/all_to_all | solution.py:71
  163.5 39.9 %all-to-all-start.4 = ((bf16[16,2,128,256]{3,2,1,0:T(8,128)(2,1)}), bf16[16,2,128,256]{3,2,1,0:T(8,128)(2,1)S(1)}, u32[]{:S(2)}, u32[]{:S(2)}) async-start(bf16[16,2,128,256]{3,2,1,0:T(8,128)(2,1)} %broadcast_select_fusion), calls=%async_computation.4 | async-start | bytes 4194304 | tf_op jit(solution)/shard_map/all_to_all | solution.py:161
  190.9 2.2 copy-start.9
  203.3 11.8 %copy-start.7 = (f32[128,8]{0,1:T(8,128)S(1)}, f32[128,8]{0,1:T(8,128)}, u32[]{:S(2)}) copy-start(f32[128,8]{0,1:T(8,128)} %param.23) | copy-start | bytes 12292
  203.3 12.5 %copy-start.8 = (s32[16]{0:T(128)S(1)}, s32[16]{0:T(128)}, u32[]{:S(2)}) copy-start(s32[16]{0:T(128)} %param.20) | copy-start | bytes 196
  203.4 91.8 %all-to-all-start.3 = ((bf16[64,24,2048]{2,1,0:T(8,128)(2,1)}), bf16[64,24,2048]{2,1,0:T(8,128)(2,1)}, u32[]{:S(2)}, u32[]{:S(2)}) async-start(bf16[64,24,2048]{2,1,0:T(8,128)(2,1)} %bitcast.67), calls=%async_computation.3 | async-start | bytes 12582912 | tf_op jit(solution)/shard_map/all_to_all | solution.py:76
